TPU v7x, 32 devices: a whole 2x2x4 slice. The times are simulated.
32 devices in a mesh: dp: 8 (over y, x, core), tensor: 4 (over z).
Axes of the slice: x: 2, y: 2, z: 4, core: 2. Of those that a mesh axis runs over, the one named last changes fastest.
Arguments:
- inputs: bfloat16 [16384, 768], P(('dp', 'tensor')), may hold values from -6 to 6
- prefix: int32 [16], P('dp'), may hold values from 102 to 512, as said below
- cotangent: bfloat16 [16384, 768], P(('dp', 'tensor')), may hold values from -6 to 6
- w_query: bfloat16 [768, 768], P('dp', 'tensor'), may hold values from -0.3125 to 0.3125
- w_key: bfloat16 [768, 768], P('dp', 'tensor'), may hold values from -0.3125 to 0.3125
- w_value: bfloat16 [768, 768], P('dp', 'tensor'), may hold values from -0.21875 to 0.21875
- w_out: bfloat16 [768, 768], P('tensor', 'dp'), may hold values from -0.875 to 0.875
- w_up: bfloat16 [768, 3072], P('dp', 'tensor'), may hold values from -0.21875 to 0.21875
- w_down: bfloat16 [3072, 768], P('tensor', 'dp'), may hold values from -0.109375 to 0.109375
- b_query: bfloat16 [768], replicated, may hold values from -3 to 3
- b_value: bfloat16 [768], replicated, may hold values from -3 to 3
- b_out: bfloat16 [768], replicated, may hold values from -2 to 2
- b_up: bfloat16 [3072], replicated, may hold values from -3 to 3
- b_down: bfloat16 [768], replicated, may hold values from -2 to 2
- gain_one: bfloat16 [768], replicated, may hold values from 0.25 to 1.75
- shift_one: bfloat16 [768], replicated, may hold values from -2 to 2
- gain_two: bfloat16 [768], replicated, may hold values from 0.25 to 1.75
- shift_two: bfloat16 [768], replicated, may hold values from -2 to 2
Outputs:
- output: bfloat16 [16384, 768], P(('dp', 'tensor'))
- grad_input: float32 [16384, 768], P(('dp', 'tensor'))
- grad_w_query: float32 [768, 768], P('dp', 'tensor')
- grad_w_key: float32 [768, 768], P('dp', 'tensor')
- grad_w_value: float32 [768, 768], P('dp', 'tensor')
- grad_w_out: float32 [768, 768], P('tensor', 'dp')
- grad_w_up: float32 [768, 3072], P('dp', 'tensor')
- grad_w_down: float32 [3072, 768], P('tensor', 'dp')
- grad_b_query: float32 [768], replicated
- grad_b_value: float32 [768], replicated
- grad_b_out: float32 [768], replicated
- grad_b_up: float32 [3072], replicated
- grad_b_down: float32 [768], replicated
- grad_gain_one: float32 [768], replicated
- grad_shift_one: float32 [768], replicated
- grad_gain_two: float32 [768], replicated
- grad_shift_two: float32 [768], replicated
Inputs may be any that keep to these rules, and one draw needn't show every extreme that they name: Every draw has a sequence whose prefix is exactly 512.
All inputs are finite; a program needn't handle non-finite values.
Results may differ from a plain program's by a relative error of at most 0.015.
Values may be sent and summed in bfloat16 or wider, within the bound.
No kernel may reach another device: no remote copies, remote signals or barrier semaphores. Data moves between devices by JAX's collectives and lax.ppermute only.
A program may use at most 192 MiB of HBM per device.

v0:
```python
import jax
import jax.numpy as jnp
from jax import lax
from jax.sharding import PartitionSpec as P

HEAD = 64
SEQ_LEN = 1024
norm_eps = 1e-12
masked_score = -1e30


def layer_norm(values, norm_gain, norm_shift):
    center = values - jnp.mean(values, axis=-1, keepdims=True)
    spread = jnp.mean(center * center, axis=-1, keepdims=True)
    return center * lax.rsqrt(spread + norm_eps) * norm_gain + norm_shift


def gelu_exact(values):
    return jax.nn.gelu(values, approximate=False)


def dot_right(first_op, second_op):
    return jnp.dot(first_op, second_op, preferred_element_type=jnp.float32)


def dot_back(first_op, second_op):
    return lax.dot_general(
        first_op, second_op, (((1,), (1,)), ((), ())), preferred_element_type=jnp.float32
    )


def dot_over_rows(first_op, second_op):
    return lax.dot_general(
        first_op, second_op, (((0,), (0,)), ((), ())), preferred_element_type=jnp.float32
    )


def block_rows():
    return min(512, SEQ_LEN)


def key_stop(begin_row, block_size):
    prefix_end = -(-(SEQ_LEN // 2) // block_size) * block_size
    return min(SEQ_LEN, max(begin_row + block_size, prefix_end))


def block_scores(queries, key_rows, lengths, begin_row, block_size, stop_key):
    scaling = HEAD ** (-0.5)
    scores = (
        jnp.einsum(
            "sqhe,skhe->shqk",
            queries[:, begin_row : begin_row + block_size],
            key_rows[:, :stop_key],
            preferred_element_type=jnp.float32,
        )
        * scaling
    )
    row_index = begin_row + lax.broadcasted_iota(jnp.int32, (block_size, stop_key), 0)
    col_index = lax.broadcasted_iota(jnp.int32, (block_size, stop_key), 1)
    visible = (col_index <= row_index)[None, None] | (
        col_index[None, None] < lengths[:, None, None, None]
    )
    return jnp.where(visible, scores, masked_score)


def attend_forward(queries, key_rows, value_rows, lengths):
    block_size = block_rows()
    outputs = []
    log_sums = []
    for begin_row in range(0, SEQ_LEN, block_size):
        stop_key = key_stop(begin_row, block_size)
        scores = block_scores(queries, key_rows, lengths, begin_row, block_size, stop_key)
        row_top = jnp.max(scores, axis=-1, keepdims=True)
        exponent = jnp.exp(scores - row_top)
        row_total = jnp.sum(exponent, axis=-1, keepdims=True)
        probability = (exponent / row_total).astype(jnp.bfloat16)
        outputs.append(
            jnp.einsum(
                "shqk,skhe->sqhe",
                probability,
                value_rows[:, :stop_key],
                preferred_element_type=jnp.float32,
            )
        )
        log_sums.append(row_top[..., 0] + jnp.log(row_total[..., 0]))
    return (jnp.concatenate(outputs, axis=1), jnp.concatenate(log_sums, axis=2))


def attend_backward(queries, key_rows, value_rows, grad_attn, log_sums, lengths):
    block_size = block_rows()
    scaling = HEAD ** (-0.5)
    grad_queries = []
    grad_keys = jnp.zeros(key_rows.shape, jnp.float32)
    grad_values = jnp.zeros(value_rows.shape, jnp.float32)
    for begin_row in range(0, SEQ_LEN, block_size):
        stop_key = key_stop(begin_row, block_size)
        scores = block_scores(queries, key_rows, lengths, begin_row, block_size, stop_key)
        probability = jnp.exp(scores - log_sums[:, :, begin_row : begin_row + block_size, None])
        grad_block = grad_attn[:, begin_row : begin_row + block_size]
        grad_prob = jnp.einsum(
            "sqhe,skhe->shqk",
            grad_block,
            value_rows[:, :stop_key],
            preferred_element_type=jnp.float32,
        )
        row_delta = jnp.sum(probability * grad_prob, axis=-1, keepdims=True)
        grad_scores = (probability * (grad_prob - row_delta)).astype(jnp.bfloat16)
        grad_queries.append(
            jnp.einsum(
                "shqk,skhe->sqhe",
                grad_scores,
                key_rows[:, :stop_key],
                preferred_element_type=jnp.float32,
            )
            * scaling
        )
        key_part = (
            jnp.einsum(
                "shqk,sqhe->skhe",
                grad_scores,
                queries[:, begin_row : begin_row + block_size],
                preferred_element_type=jnp.float32,
            )
            * scaling
        )
        grad_keys = grad_keys.at[:, :stop_key].add(key_part)
        value_part = jnp.einsum(
            "shqk,sqhe->skhe",
            probability.astype(jnp.bfloat16),
            grad_block,
            preferred_element_type=jnp.float32,
        )
        grad_values = grad_values.at[:, :stop_key].add(value_part)
    return (jnp.concatenate(grad_queries, axis=1), grad_keys, grad_values)


def placed(segment, total_width, part_index):
    empty = jnp.zeros((total_width,), jnp.float32)
    return lax.dynamic_update_slice_in_dim(empty, segment, part_index * segment.shape[0], 0)


def body(
    inputs,
    prefix,
    cotangent,
    w_query,
    w_key,
    w_value,
    w_out,
    w_up,
    w_down,
    b_query,
    b_value,
    b_out,
    b_up,
    b_down,
    gain_one,
    shift_one,
    gain_two,
    shift_two,
):
    float_type = jnp.float32
    half_type = jnp.bfloat16
    part_index = lax.axis_index("tensor")
    full_query, full_key, full_value, full_out = (
        lax.all_gather(w_query, "dp", axis=0, tiled=True),
        lax.all_gather(w_key, "dp", axis=0, tiled=True),
        lax.all_gather(w_value, "dp", axis=0, tiled=True),
        lax.all_gather(w_out, "dp", axis=1, tiled=True),
    )
    full_up, full_down = (
        lax.all_gather(w_up, "dp", axis=0, tiled=True),
        lax.all_gather(w_down, "dp", axis=1, tiled=True),
    )
    head_width = full_query.shape[1]
    ff_width = full_up.shape[1]
    heads_here = head_width // HEAD
    bias_query = lax.dynamic_slice_in_dim(
        b_query.astype(float_type), part_index * head_width, head_width
    )
    bias_value = lax.dynamic_slice_in_dim(
        b_value.astype(float_type), part_index * head_width, head_width
    )
    bias_up = lax.dynamic_slice_in_dim(b_up.astype(float_type), part_index * ff_width, ff_width)
    gain_first = gain_one.astype(float_type)
    shift_first = shift_one.astype(float_type)
    gain_second = gain_two.astype(float_type)
    shift_second = shift_two.astype(float_type)
    in_rows = inputs.astype(float_type)
    norm_first = layer_norm(in_rows, gain_first, shift_first)
    normed_one = lax.all_gather(norm_first.astype(half_type), "tensor", axis=0, tiled=True)
    seq_count = normed_one.shape[0] // SEQ_LEN
    stacked = jnp.concatenate([full_query, full_key, full_value], axis=1)
    projected = dot_right(normed_one, stacked)
    shape_four = (seq_count, SEQ_LEN, heads_here, HEAD)
    queries = (projected[:, :head_width] + bias_query).astype(half_type).reshape(shape_four)
    key_rows = projected[:, head_width : 2 * head_width].astype(half_type).reshape(shape_four)
    value_rows = (projected[:, 2 * head_width :] + bias_value).astype(half_type).reshape(shape_four)
    attended, log_sums = attend_forward(queries, key_rows, value_rows, prefix)
    attended = attended.reshape(-1, head_width).astype(half_type)
    attn_piece = lax.psum_scatter(
        dot_right(attended, full_out), "tensor", scatter_dimension=0, tiled=True
    )
    middle = in_rows + attn_piece + b_out.astype(float_type)
    norm_second = layer_norm(middle, gain_second, shift_second)
    normed_two = lax.all_gather(norm_second.astype(half_type), "tensor", axis=0, tiled=True)
    pre_act = dot_right(normed_two, full_up) + bias_up
    activated = gelu_exact(pre_act).astype(half_type)
    ff_piece = lax.psum_scatter(
        dot_right(activated, full_down).astype(jnp.bfloat16),
        "tensor",
        scatter_dimension=0,
        tiled=True,
    ).astype(jnp.float32)
    result = (middle + ff_piece + b_down.astype(float_type)).astype(half_type)
    grad_result = cotangent.astype(float_type)
    grad_ff_rows = lax.all_gather(cotangent, "tensor", axis=0, tiled=True)
    grad_act = dot_back(grad_ff_rows, full_down)
    grad_down = dot_over_rows(activated, grad_ff_rows)
    grad_pre = jax.vjp(gelu_exact, pre_act)[1](grad_act)[0].astype(half_type)
    grad_bias_up = jnp.sum(grad_pre, axis=0, dtype=float_type)
    grad_up = dot_over_rows(normed_two, grad_pre)
    grad_norm_two = lax.psum_scatter(
        dot_back(grad_pre, full_up), "tensor", scatter_dimension=0, tiled=True
    )
    norm_two_back = jax.vjp(layer_norm, middle, gain_second, shift_second)[1](grad_norm_two)
    grad_middle = grad_result + norm_two_back[0]
    grad_attn_rows = lax.all_gather(grad_middle.astype(half_type), "tensor", axis=0, tiled=True)
    grad_attended = dot_back(grad_attn_rows, full_out).astype(half_type)
    grad_out_proj = dot_over_rows(attended, grad_attn_rows)
    grad_queries, grad_keys, grad_values = attend_backward(
        queries, key_rows, value_rows, grad_attended.reshape(shape_four), log_sums, prefix
    )
    grads_joined = jnp.concatenate(
        [
            grad_queries.reshape(-1, head_width),
            grad_keys.reshape(-1, head_width),
            grad_values.reshape(-1, head_width),
        ],
        axis=1,
    ).astype(half_type)
    grad_stacked = dot_over_rows(normed_one, grads_joined)
    column_sums = jnp.sum(grads_joined, axis=0, dtype=float_type)
    grad_norm_one = lax.psum_scatter(
        dot_back(grads_joined, stacked).astype(jnp.bfloat16),
        "tensor",
        scatter_dimension=0,
        tiled=True,
    ).astype(jnp.float32)
    norm_one_back = jax.vjp(layer_norm, in_rows, gain_first, shift_first)[1](grad_norm_one)
    grad_input = grad_middle + norm_one_back[0]
    grad_query = grad_stacked[:, :head_width]
    grad_key = grad_stacked[:, head_width : 2 * head_width]
    grad_value = grad_stacked[:, 2 * head_width :]
    shard_query, shard_key, shard_value, shard_out, shard_up, shard_down = (
        lax.psum_scatter(grad_query, "dp", scatter_dimension=0, tiled=True),
        lax.psum_scatter(grad_key, "dp", scatter_dimension=0, tiled=True),
        lax.psum_scatter(grad_value, "dp", scatter_dimension=0, tiled=True),
        lax.psum_scatter(grad_out_proj, "dp", scatter_dimension=1, tiled=True),
        lax.psum_scatter(grad_up, "dp", scatter_dimension=0, tiled=True),
        lax.psum_scatter(grad_down, "dp", scatter_dimension=1, tiled=True),
    )
    vector_sums = lax.psum(
        (
            placed(column_sums[:head_width], b_query.shape[0], part_index),
            placed(column_sums[2 * head_width :], b_value.shape[0], part_index),
            jnp.sum(grad_middle, axis=0),
            placed(grad_bias_up, b_up.shape[0], part_index),
            jnp.sum(grad_result, axis=0),
            norm_one_back[1],
            norm_one_back[2],
            norm_two_back[1],
            norm_two_back[2],
        ),
        ("dp", "tensor"),
    )
    return (
        result,
        grad_input,
        shard_query,
        shard_key,
        shard_value,
        shard_out,
        shard_up,
        shard_down,
        vector_sums[0],
        vector_sums[1],
        vector_sums[2],
        vector_sums[3],
        vector_sums[4],
        vector_sums[5],
        vector_sums[6],
        vector_sums[7],
        vector_sums[8],
    )


def solution(mesh):
    placed = (
        P(("dp", "tensor"), None),
        P("dp"),
        P(("dp", "tensor"), None),
        P("dp", "tensor"),
        P("dp", "tensor"),
        P("dp", "tensor"),
        P("tensor", "dp"),
        P("dp", "tensor"),
        P("tensor", "dp"),
        P(),
        P(),
        P(),
        P(),
        P(),
        P(),
        P(),
        P(),
        P(),
    )
    return jax.shard_map(
        body,
        mesh=mesh,
        in_specs=placed,
        out_specs=(
            P(("dp", "tensor"), None),
            P(("dp", "tensor"), None),
            P("dp", "tensor"),
            P("dp", "tensor"),
            P("dp", "tensor"),
            P("tensor", "dp"),
            P("dp", "tensor"),
            P("tensor", "dp"),
            P(),
            P(),
            P(),
            P(),
            P(),
            P(),
            P(),
            P(),
            P(),
        ),
        check_vma=False,
    )
```

profile of v0, /device:TPU:0, one launch (start us, length us, event | category | flops | bytes accessed | tf_op | source)
XLA Modules:
  0.0 988.7 jit_solution(17090238682944329113)
XLA Ops:
  8.1 1.3 convert_reduce_fusion.3
  9.5 1.5 fusion.28
  13.0 2.4 fusion.27
  15.7 11.1 %all_gather.34 = bf16[192,768]{0,1:T(8,128)(2,1)S(1)} all-gather(bf16[192,96]{0,1:T(8,128)(2,1)S(1)} %copy.81), channel_id=1, replica_groups=mesh['dp'=8,'tensor'=4] {'dp'}, dimensions={1}, use_global_device_ids=true | all-gather | bytes 331776 | tf_op jit(solution)/shard_map/all_gather | solution.py:169
  26.8 9.5 all_gather.31
  36.3 8.6 all_gather.32
  44.9 9.5 all_gather.33
  56.1 1.5 fusion.14
  57.6 24.0 %all-gather.7.cloned.1.call-done = bf16[2048,768]{1,0:T(8,128)(2,1)} async-done(((bf16[512,768]{1,0:T(8,128)(2,1)}), bf16[2048,768]{1,0:T(8,128)(2,1)}) %all-gather.7.cloned.1.call-update) | async-done | bytes 3145744 | tf_op jit(solution)/shard_map/all_gather | solution.py:191
  81.7 4.1 fusion.65
  85.8 2.1 copy-done.13
  88.6 2.4 fusion.33
  94.9 4.2 fusion.83
  99.2 2.8 fusion
  102.0 1.7 copy-done
  103.9 3.3 fusion.48
  107.3 1.4 fusion.84
  109.6 1.7 copy-done.1
  113.6 3.7 fusion.85
  118.7 108.3 %reduce-scatter.19.cloned.1.call-done = f32[512,768]{1,0:T(8,128)} async-done(((f32[2048,768]{1,0:T(8,128)}), f32[512,768]{1,0:T(8,128)}) %reduce-scatter.19.cloned.1.call-update) | async-done | bytes 1572880 | tf_op jit(solution)/shard_map/reduce_scatter | solution.py:201
  227.0 1.7 fusion.78
  232.0 1.4 dynamic-slice_convert_fusion
  233.4 60.8 %all-gather.9.cloned.1.call-done = bf16[2048,768]{1,0:T(8,128)(2,1)} async-done(((bf16[512,768]{1,0:T(8,128)(2,1)}), bf16[2048,768]{1,0:T(8,128)(2,1)}) %all-gather.9.cloned.1.call-update) | async-done | bytes 3145744 | tf_op jit(solution)/shard_map/all_gather | solution.py:206
  294.2 7.5 fusion.86
  301.7 16.7 %all-gather.13.cloned.1.call-done = bf16[768,768]{0,1:T(8,128)(2,1)} async-done(((bf16[768,96]{0,1:T(8,128)(2,1)}), bf16[768,768]{0,1:T(8,128)(2,1)}) %all-gather.13.cloned.1.call-update) | async-done | bytes 1179664 | tf_op jit(solution)/shard_map/all_gather | solution.py:173
  318.4 64.9 %all-gather.15.cloned.1.call-done = bf16[2048,768]{1,0:T(8,128)(2,1)} async-done(((bf16[512,768]{1,0:T(8,128)(2,1)}), bf16[2048,768]{1,0:T(8,128)(2,1)}) %all-gather.15.cloned.1.call-update) | async-done | bytes 3145744 | tf_op jit(solution)/shard_map/all_gather | solution.py:217
  383.3 20.6 %convert_reduce_fusion = (f32[768]{0:T(1024)}, bf16[2048,768]{1,0:T(8,128)(2,1)S(1)}, f32[2048,768]{1,0:T(8,128)}) fusion(f32[2048,768]{1,0:T(8,128)} %fusion.86, f32[768]{0:T(1024)} %dynamic-slice_convert_fusion, bf16[2048,768]{1,0:T(8,128)(2,1)} %all-gather.15.cloned.1.call-done, bf16[768,768]{0,1:T(8,128)(2,1)} %all-gather.13.cloned.1.call-done), kind=kOutput, calls=%fused_computation.11 | convolution fusion | flops 2533883136 | bytes 20060160 | tf_op jit(solution)/shard_map/dot_general | solution.py:27
  403.9 1.7 copy-done.67
  405.6 4.6 fusion.87
  410.3 5.7 multiply_convert_fusion.2
  416.0 1.6 copy-done.15
  417.6 4.0 convolution_convert_fusion.1
  421.7 1.3 convert_element_type.121
  423.0 96.7 %reduce-scatter.23.cloned.1.call-done = f32[512,768]{1,0:T(8,128)} async-done(((f32[2048,768]{1,0:T(8,128)}), f32[512,768]{1,0:T(8,128)}) %reduce-scatter.23.cloned.1.call-update) | async-done | bytes 1572880 | tf_op jit(solution)/shard_map/reduce_scatter | solution.py:223
  519.7 2.6 multiply_reduce_fusion.2
  522.9 60.1 %reduce-scatter.21.cloned.1.call-done = bf16[512,768]{1,0:T(8,128)(2,1)} async-done(((bf16[2048,768]{1,0:T(8,128)(2,1)}), bf16[512,768]{1,0:T(8,128)(2,1)}) %reduce-scatter.21.cloned.1.call-update) | async-done | bytes 786448 | tf_op jit(solution)/shard_map/reduce_scatter | solution.py:209
  583.0 3.3 fusion.77
  588.9 63.1 %all-gather.17.cloned.1.call-done = bf16[2048,768]{1,0:T(8,128)(2,1)} async-done(((bf16[512,768]{1,0:T(8,128)(2,1)}), bf16[2048,768]{1,0:T(8,128)(2,1)}) %all-gather.17.cloned.1.call-update) | async-done | bytes 3145744 | tf_op jit(solution)/shard_map/all_gather | solution.py:228
  652.1 4.0 convolution_convert_fusion.2
  656.0 2.6 reshape.337
  659.2 4.0 fusion.38
  663.2 4.4 multiply_reduce_fusion.1
  667.7 2.6 multiply_convert_fusion.1
  670.3 1.4 fusion.46
  673.9 2.3 convolution_bitcast_fusion
  676.5 10.6 %multiply_reduce_fusion = (f32[2,3,512]{2,1,0:T(4,128)S(1)}, f32[2,3,512,1024]{3,2,1,0:T(8,128)}) fusion(f32[2,3,512,1024]{3,2,1,0:T(8,128)} %copy-done, f32[2,3,512]{2,1,0:T(4,128)S(1)} %log_add_fusion, bf16[2,1024,3,64]{1,0,3,2:T(2,128)(2,1)S(1)} %reshape.334, bf16[2,512,3,64]{1,0,3,2:T(2,128)(2,1)S(1)} %get-tuple-element.165), kind=kOutput, calls=%fused_computation.1 | convolution fusion | flops 412087296 | bytes 26370048 | tf_op jit(solution)/shard_map/sqhe,skhe->shqk/dot_general | solution.py:100
  687.1 6.0 fusion.34
  694.2 6.4 multiply_convert_fusion
  700.6 2.0 fusion.47
  707.1 4.5 convolution_convert_fusion
  711.9 6.9 fusion.89
  718.9 6.9 fusion.88
  725.9 3.9 fusion.90
  733.9 2.2 convert_reduce_fusion.1
  736.4 1.6 copy.106
  738.1 34.4 %reduce-scatter.25.cloned.1.call-done = bf16[512,768]{1,0:T(8,128)(2,1)} async-done(((bf16[2048,768]{1,0:T(8,128)(2,1)}), bf16[512,768]{1,0:T(8,128)(2,1)}) %reduce-scatter.25.cloned.1.call-update) | async-done | bytes 786448 | tf_op jit(solution)/shard_map/reduce_scatter | solution.py:244
  772.5 1.8 convert_reduce_fusion.2
  774.3 2.1 fusion.31
  776.4 2.0 convert_reduce_fusion.4
  778.4 41.5 %all-reduce.2 = (f32[768]{0:T(1024)}, f32[768]{0:T(1024)}, f32[768]{0:T(1024)}, f32[3072]{0:T(1024)}, f32[768]{0:T(1024)}, /*index=5*/f32[768]{0:T(1024)}, f32[768]{0:T(1024)}, f32[768]{0:T(1024)}, f32[768]{0:T(1024)}) all-reduce(f32[768]{0:T(1024)S(1)} %slice_dynamic-update-slice_fusion.1, ...), channel_id=1, replica_groups=mesh['dp'=8,'tensor'=4] {'dp','tensor'}, use_global_device_ids=true, to_apply=%region_25.26 | all-reduce | flops 9216 | bytes 73728 | tf_op jit(solution)/shard_map/psum | solution.py:263
  819.9 45.2 %reduce-scatter.27.cloned.1.call-done = f32[96,768]{1,0:T(8,128)} async-done(((f32[768,768]{1,0:T(8,128)}), f32[96,768]{1,0:T(8,128)}) %reduce-scatter.27.cloned.1.call-update) | async-done | bytes 294928 | tf_op jit(solution)/shard_map/reduce_scatter | solution.py:260
  865.2 38.5 %reduce-scatter.35.cloned.1.call-done = f32[96,192]{1,0:T(8,128)} async-done(((f32[768,192]{1,0:T(8,128)}), f32[96,192]{1,0:T(8,128)}) %reduce-scatter.35.cloned.1.call-update) | async-done | bytes 73744
  903.7 38.7 %reduce-scatter.33.cloned.1.call-done = f32[96,192]{1,0:T(8,128)} async-done(((f32[768,192]{1,0:T(8,128)}), f32[96,192]{1,0:T(8,128)}) %reduce-scatter.33.cloned.1.call-update) | async-done | bytes 73744
  942.4 38.5 %reduce-scatter.31.cloned.1.call-done = f32[96,192]{1,0:T(8,128)} async-done(((f32[768,192]{1,0:T(8,128)}), f32[96,192]{1,0:T(8,128)}) %reduce-scatter.31.cloned.1.call-update) | async-done | bytes 73744
  (238 shorter events, 33.0 us)
Async XLA Ops:
  8.0 7.4 copy-start.63
  8.0 7.5 copy-start.64
  8.0 7.5 copy-start.48
  8.1 18.7 %copy-start.45 = (bf16[96,192]{1,0:T(8,128)(2,1)S(1)}, bf16[96,192]{1,0:T(8,128)(2,1)}, u32[]{:S(2)}) copy-start(bf16[96,192]{1,0:T(8,128)(2,1)} %param.33) | copy-start | bytes 110596
  8.1 28.2 %copy-start.46 = (bf16[96,192]{1,0:T(8,128)(2,1)S(1)}, bf16[96,192]{1,0:T(8,128)(2,1)}, u32[]{:S(2)}) copy-start(bf16[96,192]{1,0:T(8,128)(2,1)} %param.34) | copy-start | bytes 110596
  8.1 36.8 %copy-start.47 = (bf16[96,192]{1,0:T(8,128)(2,1)S(1)}, bf16[96,192]{1,0:T(8,128)(2,1)}, u32[]{:S(2)}) copy-start(bf16[96,192]{1,0:T(8,128)(2,1)} %param.35) | copy-start | bytes 110596
  8.1 46.8 %copy-start.62 = (s32[2]{0:T(128)S(1)}, s32[2]{0:T(128)}, u32[]{:S(2)}) copy-start(s32[2]{0:T(128)} %param.31) | copy-start | bytes 28
  8.1 73.6 %all-gather.7.cloned.1.call-start = ((), (), s32[]{:S(2)}) async-start(), calls=%async_computation.10 | async-start | bytes 3932160 | tf_op jit(solution)/shard_map/all_gather | solution.py:191
  9.5 6.0 copy-start.35
  11.6 3.9 copy-start.49
  12.3 3.2 copy-start.33
  15.3 211.6 %reduce-scatter.19.cloned.1.call-start = ((), (), s32[]{:S(2)}) async-start(), calls=%async_computation.11 | async-start | bytes 7864320 | tf_op jit(solution)/shard_map/reduce_scatter | solution.py:201
  36.3 45.4 %copy-start.26 = (bf16[768,192]{1,0:T(8,128)(2,1)}, bf16[768,192]{1,0:T(8,128)(2,1)S(1)}, u32[]{:S(2)}) copy-start(bf16[768,192]{1,0:T(8,128)(2,1)S(1)} %all_gather.31) | copy-start | bytes 884740
  44.9 36.8 %copy-start.28 = (bf16[768,192]{1,0:T(8,128)(2,1)}, bf16[768,192]{1,0:T(8,128)(2,1)S(1)}, u32[]{:S(2)}) copy-start(bf16[768,192]{1,0:T(8,128)(2,1)S(1)} %all_gather.32) | copy-start | bytes 884740
  54.4 31.3 %copy-start.30 = (bf16[768,192]{1,0:T(8,128)(2,1)}, bf16[768,192]{1,0:T(8,128)(2,1)S(1)}, u32[]{:S(2)}) copy-start(bf16[768,192]{1,0:T(8,128)(2,1)S(1)} %all_gather.33) | copy-start | bytes 884740
  88.6 6.3 copy-start.5
  94.9 4.3 copy-start.16
  94.9 12.3 %copy-start.22 = (bf16[2,512,3,64]{1,0,3,2:T(2,128)(2,1)}, bf16[2,512,3,64]{1,0,3,2:T(2,128)(2,1)S(1)}, u32[]{:S(2)}) copy-start(bf16[2,512,3,64]{1,0,3,2:T(2,128)(2,1)S(1)} %get-tuple-element.166) | copy-start | bytes 1179652
  99.2 4.5 copy-start
  99.2 4.7 copy-start.37
  103.9 3.3 copy-start.39
  103.9 3.3 copy-start.20
  103.9 3.3 copy-start.25
  108.7 2.7 copy-start.41
  108.7 2.7 copy-start.18
  113.6 3.7 copy-start.10
  117.4 109.6 %copy-start.2 = (bf16[512,768]{1,0:T(8,128)(2,1)S(1)}, bf16[512,768]{1,0:T(8,128)(2,1)}, u32[]{:S(2)}) copy-start(bf16[512,768]{1,0:T(8,128)(2,1)} %param.30) | copy-start | bytes 2359300
  117.4 116.0 %all-gather.11.cloned.1.call-start = ((), (), s32[]{:S(2)}) async-start(), calls=%async_computation.13 | async-start | bytes 1327104 | tf_op jit(solution)/shard_map/all_gather | solution.py:172
  118.0 176.2 %all-gather.9.cloned.1.call-start = ((), (), s32[]{:S(2)}) async-start(), calls=%async_computation.12 | async-start | bytes 3932160 | tf_op jit(solution)/shard_map/all_gather | solution.py:206
  230.2 88.1 %all-gather.13.cloned.1.call-start = ((), (), s32[]{:S(2)}) async-start(), calls=%async_computation.14 | async-start | bytes 1327104 | tf_op jit(solution)/shard_map/all_gather | solution.py:173
  230.8 152.5 %all-gather.15.cloned.1.call-start = ((), (), s32[]{:S(2)}) async-start(), calls=%async_computation.16 | async-start | bytes 3932160 | tf_op jit(solution)/shard_map/all_gather | solution.py:217
  231.6 288.1 %reduce-scatter.23.cloned.1.call-start = ((), (), s32[]{:S(2)}) async-start(), calls=%async_computation.17 | async-start | bytes 7864320 | tf_op jit(solution)/shard_map/reduce_scatter | solution.py:223
  383.3 22.3 %copy-start.65 = (bf16[768,768]{1,0:T(8,128)(2,1)S(1)}, bf16[768,768]{1,0:T(8,128)(2,1)}, u32[]{:S(2)}) copy-start(bf16[768,768]{1,0:T(8,128)(2,1)} %all-gather.11.cloned.1.call-done) | copy-start | bytes 3538948
  410.2 172.7 %reduce-scatter.21.cloned.1.call-start = ((), (), s32[]{:S(2)}) async-start(), calls=%async_computation.15 | async-start | bytes 3932160 | tf_op jit(solution)/shard_map/reduce_scatter | solution.py:209
  410.3 7.3 copy-start.66
  421.6 230.4 %all-gather.17.cloned.1.call-start = ((), (), s32[]{:S(2)}) async-start(), calls=%async_computation.18 | async-start | bytes 3932160 | tf_op jit(solution)/shard_map/all_gather | solution.py:228
  583.0 4.4 copy-start.8
  586.3 69.7 %copy-start.53 = (f32[512]{0:T(512)}, f32[512]{0:T(512)S(1)}, u32[]{:S(2)}) copy-start(f32[512]{0:T(512)S(1)} %negate_multiply_fusion.2) | copy-start | bytes 6148
  588.6 147.8 %reduce-scatter.37.cloned.1.call-start = ((), (), s32[]{:S(2)}) async-start(), calls=%async_computation.25 | async-start | bytes 884736
  588.9 74.3 %copy-start.32 = (f32[2,3,512]{2,1,0:T(4,128)}, f32[2,3,512]{2,1,0:T(4,128)S(1)}, u32[]{:S(2)}) copy-start(f32[2,3,512]{2,1,0:T(4,128)S(1)} %log_add_fusion.1) | copy-start | bytes 36868
  659.2 4.0 copy-start.19
  659.2 8.5 slice-start.3
  663.2 4.4 slice-start.4
  667.6 2.6 copy-start.21
  676.2 96.3 %reduce-scatter.25.cloned.1.call-start = ((), (), s32[]{:S(2)}) async-start(), calls=%async_computation.19 | async-start | bytes 3932160 | tf_op jit(solution)/shard_map/reduce_scatter | solution.py:244
  676.5 17.7 %slice-start = ((s8[12582912]{0:T(1024)(128)(4,1)}), s8[4194304]{0:T(1024)(128)(4,1)S(1)}, s32[]{:S(2)}) async-start(s8[12582912]{0:T(1024)(128)(4,1)} %bitcast.80), calls=%async_computation.26 | async-start | bytes 8388608
  676.5 17.7 %slice-start.1 = ((s8[12582912]{0:T(1024)(128)(4,1)}), s8[4194304]{0:T(1024)(128)(4,1)S(1)}, s32[]{:S(2)}) async-start(s8[12582912]{0:T(1024)(128)(4,1)} %bitcast.80), calls=%async_computation.27 | async-start | bytes 8388608
  687.1 7.1 slice-start.2
  694.2 6.4 copy-start.6
  707.1 18.8 %copy-start.12 = (bf16[2048,576]{0,1:T(8,128)(2,1)}, bf16[2048,576]{0,1:T(8,128)(2,1)S(1)}, u32[]{:S(2)}) copy-start(bf16[2048,576]{0,1:T(8,128)(2,1)S(1)} %constant_dynamic-update-slice_fusion) | copy-start | bytes 7077892
  711.6 108.3 %reduce-scatter.29.cloned.1.call-start = ((), (), s32[]{:S(2)}) async-start(), calls=%async_computation.21 | async-start | bytes 2654208 | tf_op jit(solution)/shard_map/reduce_scatter | solution.py:261
  718.9 146.3 %reduce-scatter.27.cloned.1.call-start = ((), (), s32[]{:S(2)}) async-start(), calls=%async_computation.20 | async-start | bytes 2654208 | tf_op jit(solution)/shard_map/reduce_scatter | solution.py:260
  725.8 177.8 %reduce-scatter.35.cloned.1.call-start = ((), (), s32[]{:S(2)}) async-start(), calls=%async_computation.24 | async-start | bytes 884736
  729.8 2.6 copy-start.58
  731.1 211.2 %reduce-scatter.33.cloned.1.call-start = ((), (), s32[]{:S(2)}) async-start(), calls=%async_computation.23 | async-start | bytes 884736
  731.2 41.3 %copy-start.34 = (f32[768]{0:T(1024)S(1)}, f32[768]{0:T(1024)}, u32[]{:S(2)}) copy-start(f32[768]{0:T(1024)} %copy-done.33) | copy-start | bytes 9220
  731.2 41.3 %copy-start.36 = (f32[512]{0:T(512)S(1)}, f32[512]{0:T(512)}, u32[]{:S(2)}) copy-start(f32[512]{0:T(512)} %copy-done.35) | copy-start | bytes 6148
  732.4 248.5 %reduce-scatter.31.cloned.1.call-start = ((), (), s32[]{:S(2)}) async-start(), calls=%async_computation.22 | async-start | bytes 884736
  732.7 41.5 %copy-start.52 = (f32[512]{0:T(512)S(1)}, f32[512]{0:T(512)}, u32[]{:S(2)}) copy-start(f32[512]{0:T(512)} %copy-done.51) | copy-start | bytes 6148
  732.7 41.5 %copy-start.50 = (f32[512]{0:T(512)S(1)}, f32[512]{0:T(512)}, u32[]{:S(2)}) copy-start(f32[512]{0:T(512)} %copy-done.49) | copy-start | bytes 6148
  733.9 42.5 %copy-start.4 = (f32[512,768]{1,0:T(8,128)S(1)}, f32[512,768]{1,0:T(8,128)}, u32[]{:S(2)}) copy-start(f32[512,768]{1,0:T(8,128)} %copy-done.3) | copy-start | bytes 4718596
  733.9 42.5 %copy-start.9 = (bf16[512,768]{1,0:T(8,128)(2,1)S(1)}, bf16[512,768]{1,0:T(8,128)(2,1)}, u32[]{:S(2)}) copy-start(bf16[512,768]{1,0:T(8,128)(2,1)} %param.32) | copy-start | bytes 2359300
  733.9 42.5 %copy-start.54 = (f32[512]{0:T(512)S(1)}, f32[512]{0:T(512)}, u32[]{:S(2)}) copy-start(f32[512]{0:T(512)} %copy-done.53) | copy-start | bytes 6148
  772.5 3.9 copy-start.7
  (25 other events, 40.9 us)
Sparse Core Ops, SparseCore 0:
  15.5 66.1 all-gather.6
  117.5 109.4 reduce-scatter.18
  588.7 63.2 all-gather.16
Sparse Core Ops, SparseCore 1:
  119.8 22.4 all-gather.10
  230.3 63.8 all-gather.8
  295.9 22.4 all-gather.12
  320.0 63.3 all-gather.14
  410.3 109.3 reduce-scatter.22
  522.0 60.9 reduce-scatter.20
  676.3 33.5 reduce-scatter.36
  712.0 60.4 reduce-scatter.24
  776.3 42.3 reduce-scatter.28
  822.6 42.5 reduce-scatter.26
  868.8 34.9 reduce-scatter.34
  907.4 34.9 reduce-scatter.32
  945.9 34.9 reduce-scatter.30
where the time goes:
time: 997 us; the launch traced here: 989 us
  waiting for transfers between devices  692 us (69%)
  matrix products  114 us (11%)
  blocking collectives  80.2 us (8%)
  other arithmetic  53 us (5%)
  local copies, waits for them, and re-layouts  30.8 us (3%)
  between operations  17.1 us (2%)
    unnamed x20, waiting for transfers between devices  118 us
    reduce_scatter x1, waiting for transfers between devices, body(): lax.psum_scatter(dot_right(attended, full_out), 'tensor', scatter_dimensi...  108 us
    reduce_scatter x1, waiting for transfers between devices, body(): lax.psum_scatter(dot_back(grad_pre, full_up), 'tensor', scatter_dimension...  96.7 us
    all_gather x1, waiting for transfers between devices, body(): grad_ff_rows = lax.all_gather(cotangent, 'tensor', axis=0, tiled=True)  64.9 us
    all_gather x1, waiting for transfers between devices, body(): lax.all_gather(grad_middle.astype(half_type), 'tensor', axis=0, tiled=True)  63.1 us
    all_gather x1, waiting for transfers between devices, body(): lax.all_gather(norm_second.astype(half_type), 'tensor', axis=0, tiled=True)  60.8 us
    reduce_scatter x1, waiting for transfers between devices, body(): lax.psum_scatter(dot_right(activated, full_down).astype(jnp.bfloat16), 't...  60.1 us
    reduce_scatter x1, waiting for transfers between devices, body(): lax.psum_scatter(grad_up, 'dp', scatter_dimension=0, tiled=True)  45.2 us
  transfers between devices with their start and end apart: 16, of which 13 were waited for; matrix products, arithmetic and copies ran while one was open for 10% of the time, Pallas kernels for 0%

commit v1 on v0

--- a/solution.py
+++ b/solution.py
@@ -214,7 +214,20 @@
     ).astype(jnp.float32)
     result = (middle + ff_piece + b_down.astype(float_type)).astype(half_type)
     grad_result = cotangent.astype(float_type)
-    grad_ff_rows = lax.all_gather(cotangent, "tensor", axis=0, tiled=True)
+    n_peers_all = jax.lax.axis_size("tensor")
+    series = [cotangent]
+    pp = 1
+    while pp < n_peers_all:
+        met_up = jax.lax.ppermute(
+            series[pp - 1],
+            axis_name="tensor",
+            perm=[(h, (h - 1) % n_peers_all) for h in range(n_peers_all)],
+        )
+        series.append(met_up)
+        pp += 1
+    z1 = jnp.concatenate(series, 0)
+    w2 = jax.lax.axis_index("tensor")
+    grad_ff_rows = jnp.roll(z1, w2 * cotangent.shape[0], 0)
     grad_act = dot_back(grad_ff_rows, full_down)
     grad_down = dot_over_rows(activated, grad_ff_rows)
     grad_pre = jax.vjp(gelu_exact, pre_act)[1](grad_act)[0].astype(half_type)

time: 997 us -> 967 us (0.970)
  waiting for transfers between devices: 692 us -> 642 us
  local copies, waits for them, and re-layouts: 30.8 us -> 45 us
    ppermute x0 -> x3, waiting for transfers between devices: none -> 95.3 us  [body(): jax.lax.ppermute(series[pp - 1], axis_name='tensor', perm=[(h, (h - 1) %...]
    all_gather x1 -> x0, waiting for transfers between devices: 64.9 us -> none  [body(): grad_ff_rows = lax.all_gather(cotangent, 'tensor', axis=0, tiled=True)]
    all_gather x1, waiting for transfers between devices: 60.8 us -> 0.01 us  [body(): lax.all_gather(norm_second.astype(half_type), 'tensor', axis=0, tiled=True)]
    reduce_scatter x1, waiting for transfers between devices: 45.2 us -> 0.01 us  [body(): lax.psum_scatter(grad_up, 'dp', scatter_dimension=0, tiled=True)]
    reduce_scatter x1, waiting for transfers between devices: 0.01 us -> 44 us  [body(): lax.psum_scatter(grad_down, 'dp', scatter_dimension=1, tiled=True)]
    all_gather x1, waiting for transfers between devices: 16.7 us -> 0.01 us  [body(): lax.all_gather(w_down, 'dp', axis=1, tiled=True)]
    dot_general x4, matrix products: 19.3 us -> 33.7 us  [dot_right(): return jnp.dot(first_op, second_op, preferred_element_type=jnp.float32)]
    unnamed x157 -> x152, local copies, waits for them, and re-layouts: 19 us -> 30.9 us
  transfers between devices with their start and end apart: 16 -> 18, of which waited for: 13 -> 13; matrix products, arithmetic and copies ran while one was open for 10% -> 13% of each run, Pallas kernels for 0% -> 0%
where the time goes in v1:
time: 967 us; the launch traced here: 958 us
  waiting for transfers between devices  642 us (66%)
  matrix products  120 us (12%)
  blocking collectives  80.1 us (8%)
  other arithmetic  49.5 us (5%)
  local copies, waits for them, and re-layouts  45 us (5%)
  between operations  16.8 us (2%)
    unnamed x19, waiting for transfers between devices  117 us
    reduce_scatter x1, waiting for transfers between devices, body(): lax.psum_scatter(dot_right(attended, full_out), 'tensor', scatter_dimensi...  108 us
    reduce_scatter x1, waiting for transfers between devices, body(): lax.psum_scatter(dot_back(grad_pre, full_up), 'tensor', scatter_dimension...  103 us
    ppermute x3, waiting for transfers between devices, body(): jax.lax.ppermute(series[pp - 1], axis_name='tensor', perm=[(h, (h - 1) %...  95.3 us
    all_gather x1, waiting for transfers between devices, body(): lax.all_gather(grad_middle.astype(half_type), 'tensor', axis=0, tiled=True)  61.3 us
    reduce_scatter x1, waiting for transfers between devices, body(): lax.psum_scatter(dot_right(activated, full_down).astype(jnp.bfloat16), 't...  60.1 us
    reduce_scatter x1, waiting for transfers between devices, body(): lax.psum_scatter(grad_down, 'dp', scatter_dimension=1, tiled=True)  44 us
    psum x1, blocking collectives, body(): lax.psum((placed(column_sums[:head_width], b_query.shape[0], part_index),...  41.4 us
  transfers between devices with their start and end apart: 18, of which 13 were waited for; matrix products, arithmetic and copies ran while one was open for 13% of the time, Pallas kernels for 0%

profile of v1, /device:TPU:0, one launch (start us, length us, event | category | flops | bytes accessed | tf_op | source)
XLA Modules:
  0.0 957.7 jit_solution(9549794784340697657)
XLA Ops:
  9.4 1.5 fusion.34
  12.9 2.4 fusion.33
  17.8 11.1 %all_gather.31 = bf16[192,768]{0,1:T(8,128)(2,1)S(1)} all-gather(bf16[192,96]{0,1:T(8,128)(2,1)S(1)} %copy.81), channel_id=1, replica_groups=mesh['dp'=8,'tensor'=4] {'dp'}, dimensions={1}, use_global_device_ids=true | all-gather | bytes 331776 | tf_op jit(solution)/shard_map/all_gather | solution.py:169
  28.8 9.5 all_gather.28
  38.4 8.6 all_gather.29
  47.0 9.5 all_gather.30
  58.2 1.5 fusion.14
  59.7 21.9 %all-gather.6.cloned.1.call-done = bf16[2048,768]{1,0:T(8,128)(2,1)} async-done(((bf16[512,768]{1,0:T(8,128)(2,1)}), bf16[2048,768]{1,0:T(8,128)(2,1)}) %all-gather.6.cloned.1.call-update) | async-done | bytes 3145744 | tf_op jit(solution)/shard_map/all_gather | solution.py:191
  81.6 4.1 fusion.71
  85.7 2.1 copy-done.13
  88.6 2.4 fusion.39
  95.0 4.2 fusion.91
  99.3 2.8 fusion
  102.1 1.6 copy-done
  104.0 3.3 fusion.54
  113.7 3.7 fusion.93
  118.7 108.3 %reduce-scatter.19.cloned.1.call-done = f32[512,768]{1,0:T(8,128)} async-done(((f32[2048,768]{1,0:T(8,128)}), f32[512,768]{1,0:T(8,128)}) %reduce-scatter.19.cloned.1.call-update) | async-done | bytes 1572880 | tf_op jit(solution)/shard_map/reduce_scatter | solution.py:201
  227.0 1.7 fusion.86
  230.3 2.6 collective-permute-start
  233.0 35.0 %collective-permute-done = bf16[512,768]{1,0:T(8,128)(2,1)S(1)} collective-permute-done((bf16[512,768]{1,0:T(8,128)(2,1)S(1)}, bf16[512,768]{1,0:T(8,128)(2,1)S(1)}, u32[]{:S(2)}, u32[]{:S(2)}) %collective-permute-start) | collective-permute-done | bytes 786464 | tf_op jit(solution)/shard_map/ppermute | solution.py:221
  268.9 48.2 %collective-permute-done.1 = bf16[512,768]{1,0:T(8,128)(2,1)} collective-permute-done((bf16[512,768]{1,0:T(8,128)(2,1)S(1)}, bf16[512,768]{1,0:T(8,128)(2,1)}, u32[]{:S(2)}, u32[]{:S(2)}) %collective-permute-start.1) | collective-permute-done | bytes 786464 | tf_op jit(solution)/shard_map/ppermute | solution.py:221
  317.2 1.4 dynamic-slice_convert_fusion
  319.6 2.1 constant_dynamic-update-slice_fusion.6
  321.7 2.1 constant_dynamic-update-slice_fusion.5
  323.7 12.0 %collective-permute-done.2 = bf16[512,768]{1,0:T(8,128)(2,1)} collective-permute-done((bf16[512,768]{1,0:T(8,128)(2,1)}, bf16[512,768]{1,0:T(8,128)(2,1)}, u32[]{:S(2)}, u32[]{:S(2)}) %collective-permute-start.2) | collective-permute-done | bytes 786464 | tf_op jit(solution)/shard_map/ppermute | solution.py:221
  335.8 2.1 constant_dynamic-update-slice_fusion.4
  339.7 2.1 constant_dynamic-update-slice_fusion.1
  341.8 2.1 constant_dynamic-update-slice_fusion
  343.9 19.4 %multiply_convert_fusion.2 = (bf16[2048,768]{1,0:T(8,128)(2,1)}, f32[2048,768]{1,0:T(8,128)}, f32[2048,768]{1,0:T(8,128)}) fusion(f32[768]{0:T(1024)} %dynamic-slice_convert_fusion, bf16[2048,768]{1,0:T(8,128)(2,1)} %all-gather.8.cloned.1.call-done, bf16[768,768]{1,0:T(8,128)(2,1)} %all-gather.10.cloned.1.call-done), kind=kOutput, calls=%fused_computation.17 | convolution fusion | flops 2519728128 | bytes 20057088 | tf_op jit(solution)/shard_map/dot_general | solution.py:23
  363.3 11.1 %convert_reduce_fusion = (f32[768]{0:T(1024)}, bf16[2048,768]{1,0:T(8,128)(2,1)S(1)}) fusion(f32[2048,768]{1,0:T(8,128)} %get-tuple-element.153, bf16[768,768]{0,1:T(8,128)(2,1)} %all-gather.12.cloned.1.call-done, bf16[4096,768]{1,0:T(8,128)(2,1)} %constant_dynamic-update-slice_fusion, s32[]{:T(128)S(6)} %select_n.38, f32[2048,768]{1,0:T(8,128)} %get-tuple-element.171, ...), kind=kOutput, calls=%fused_computation.11 | convolution fusion | flops 2442657024 | bytes 20061188 | tf_op jit(solution)/shard_map/dot_general | solution.py:27
  374.4 1.6 copy-done.61
  376.0 4.5 fusion.94
  380.7 6.6 convolution_convert_fusion.1
  388.8 103.2 %reduce-scatter.23.cloned.1.call-done = f32[512,768]{1,0:T(8,128)} async-done(((f32[2048,768]{1,0:T(8,128)}), f32[512,768]{1,0:T(8,128)}) %reduce-scatter.23.cloned.1.call-update) | async-done | bytes 1572880 | tf_op jit(solution)/shard_map/reduce_scatter | solution.py:236
  492.0 2.6 multiply_reduce_fusion.2
  495.2 60.1 %reduce-scatter.21.cloned.1.call-done = bf16[512,768]{1,0:T(8,128)(2,1)} async-done(((bf16[2048,768]{1,0:T(8,128)(2,1)}), bf16[512,768]{1,0:T(8,128)(2,1)}) %reduce-scatter.21.cloned.1.call-update) | async-done | bytes 786448 | tf_op jit(solution)/shard_map/reduce_scatter | solution.py:209
  555.3 3.2 fusion.84
  563.0 61.3 %all-gather.14.cloned.1.call-done = bf16[2048,768]{1,0:T(8,128)(2,1)} async-done(((bf16[512,768]{1,0:T(8,128)(2,1)}), bf16[2048,768]{1,0:T(8,128)(2,1)}) %all-gather.14.cloned.1.call-update) | async-done | bytes 3145744 | tf_op jit(solution)/shard_map/all_gather | solution.py:241
  624.3 3.1 convolution_convert_fusion.2
  628.5 4.0 fusion.44
  632.6 4.4 multiply_reduce_fusion.1
  637.0 1.8 multiply_convert_fusion.1
  640.3 3.0 fusion.47
  643.2 2.3 convolution_bitcast_fusion
  645.8 10.6 %multiply_reduce_fusion = (f32[2,3,512]{2,1,0:T(4,128)S(1)}, f32[2,3,512,1024]{3,2,1,0:T(8,128)}) fusion(f32[2,3,512,1024]{3,2,1,0:T(8,128)} %copy-done, f32[2,3,512]{2,1,0:T(4,128)S(1)} %log_add_fusion, bf16[2,1024,3,64]{1,0,3,2:T(2,128)(2,1)S(1)} %copy-done.7, bf16[2,512,3,64]{1,0,3,2:T(2,128)(2,1)S(1)} %get-tuple-element.164), kind=kOutput, calls=%fused_computation.1 | convolution fusion | flops 412087296 | bytes 26370048 | tf_op jit(solution)/shard_map/sqhe,skhe->shqk/dot_general | solution.py:100
  656.4 6.0 fusion.40
  663.5 6.4 multiply_convert_fusion
  669.9 2.0 fusion.53
  677.1 4.5 convolution_convert_fusion
  681.9 7.0 fusion.95
  689.0 6.9 fusion.19
  696.0 4.6 fusion.96
  704.3 2.3 copy.99
  706.6 2.1 convert_reduce_fusion.1
  708.9 1.6 copy.106
  710.6 31.2 %reduce-scatter.25.cloned.1.call-done = bf16[512,768]{1,0:T(8,128)(2,1)} async-done(((bf16[2048,768]{1,0:T(8,128)(2,1)}), bf16[512,768]{1,0:T(8,128)(2,1)}) %reduce-scatter.25.cloned.1.call-update) | async-done | bytes 786448 | tf_op jit(solution)/shard_map/reduce_scatter | solution.py:257
  741.8 1.7 convert_reduce_fusion.2
  743.5 2.1 fusion.37
  745.6 3.1 convert_reduce_fusion.4
  748.8 41.4 %all-reduce.2 = (f32[768]{0:T(1024)}, f32[768]{0:T(1024)}, f32[768]{0:T(1024)}, f32[3072]{0:T(1024)}, f32[768]{0:T(1024)}, /*index=5*/f32[768]{0:T(1024)}, f32[768]{0:T(1024)}, f32[768]{0:T(1024)}, f32[768]{0:T(1024)}) all-reduce(f32[768]{0:T(1024)S(1)} %slice_dynamic-update-slice_fusion.1, ...), channel_id=1, replica_groups=mesh['dp'=8,'tensor'=4] {'dp','tensor'}, use_global_device_ids=true, to_apply=%region_25.26 | all-reduce | flops 9216 | bytes 73728 | tf_op jit(solution)/shard_map/psum | solution.py:276
  790.2 44.0 %reduce-scatter.29.cloned.1.call-done = f32[768,96]{0,1:T(8,128)} async-done(((f32[768,768]{0,1:T(8,128)}), f32[768,96]{0,1:T(8,128)}) %reduce-scatter.29.cloned.1.call-update) | async-done | bytes 294928 | tf_op jit(solution)/shard_map/reduce_scatter | solution.py:274
  834.2 38.7 %reduce-scatter.35.cloned.1.call-done = f32[96,192]{1,0:T(8,128)} async-done(((f32[768,192]{1,0:T(8,128)}), f32[96,192]{1,0:T(8,128)}) %reduce-scatter.35.cloned.1.call-update) | async-done | bytes 73744
  872.9 38.6 %reduce-scatter.33.cloned.1.call-done = f32[96,192]{1,0:T(8,128)} async-done(((f32[768,192]{1,0:T(8,128)}), f32[96,192]{1,0:T(8,128)}) %reduce-scatter.33.cloned.1.call-update) | async-done | bytes 73744
  911.4 38.7 %reduce-scatter.31.cloned.1.call-done = f32[96,192]{1,0:T(8,128)} async-done(((f32[768,192]{1,0:T(8,128)}), f32[96,192]{1,0:T(8,128)}) %reduce-scatter.31.cloned.1.call-update) | async-done | bytes 73744
  (236 shorter events, 45.1 us)
Async XLA Ops:
  8.0 20.8 %copy-start.43 = (bf16[96,192]{1,0:T(8,128)(2,1)S(1)}, bf16[96,192]{1,0:T(8,128)(2,1)}, u32[]{:S(2)}) copy-start(bf16[96,192]{1,0:T(8,128)(2,1)} %param.33) | copy-start | bytes 110596
  8.0 30.3 %copy-start.44 = (bf16[96,192]{1,0:T(8,128)(2,1)S(1)}, bf16[96,192]{1,0:T(8,128)(2,1)}, u32[]{:S(2)}) copy-start(bf16[96,192]{1,0:T(8,128)(2,1)} %param.34) | copy-start | bytes 110596
  8.0 38.9 %copy-start.45 = (bf16[96,192]{1,0:T(8,128)(2,1)S(1)}, bf16[96,192]{1,0:T(8,128)(2,1)}, u32[]{:S(2)}) copy-start(bf16[96,192]{1,0:T(8,128)(2,1)} %param.35) | copy-start | bytes 110596
  8.1 48.9 %copy-start.59 = (s32[2]{0:T(128)S(1)}, s32[2]{0:T(128)}, u32[]{:S(2)}) copy-start(s32[2]{0:T(128)} %param.31) | copy-start | bytes 28
  8.1 73.6 %all-gather.6.cloned.1.call-start = ((), (), s32[]{:S(2)}) async-start(), calls=%async_computation.10 | async-start | bytes 3932160 | tf_op jit(solution)/shard_map/all_gather | solution.py:191
  9.4 6.7 copy-start.37
  11.5 4.6 copy-start.46
  12.2 3.9 copy-start.35
  15.3 211.7 %reduce-scatter.19.cloned.1.call-start = ((), (), s32[]{:S(2)}) async-start(), calls=%async_computation.11 | async-start | bytes 7864320 | tf_op jit(solution)/shard_map/reduce_scatter | solution.py:201
  38.4 47.3 %copy-start.27 = (bf16[768,192]{1,0:T(8,128)(2,1)}, bf16[768,192]{1,0:T(8,128)(2,1)S(1)}, u32[]{:S(2)}) copy-start(bf16[768,192]{1,0:T(8,128)(2,1)S(1)} %all_gather.28) | copy-start | bytes 884740
  47.0 38.8 %copy-start.29 = (bf16[768,192]{1,0:T(8,128)(2,1)}, bf16[768,192]{1,0:T(8,128)(2,1)S(1)}, u32[]{:S(2)}) copy-start(bf16[768,192]{1,0:T(8,128)(2,1)S(1)} %all_gather.29) | copy-start | bytes 884740
  56.5 29.2 %copy-start.31 = (bf16[768,192]{1,0:T(8,128)(2,1)}, bf16[768,192]{1,0:T(8,128)(2,1)S(1)}, u32[]{:S(2)}) copy-start(bf16[768,192]{1,0:T(8,128)(2,1)S(1)} %all_gather.30) | copy-start | bytes 884740
  88.6 6.4 copy-start.8
  91.6 10.5 %copy-start.6 = (bf16[2,1024,3,64]{1,0,3,2:T(2,128)(2,1)}, bf16[2,1024,3,64]{1,0,3,2:T(2,128)(2,1)S(1)}, u32[]{:S(2)}) copy-start(bf16[2,1024,3,64]{1,0,3,2:T(2,128)(2,1)S(1)} %reshape.334) | copy-start | bytes 2359300
  95.0 4.3 copy-start.18
  95.0 12.3 %copy-start.24 = (bf16[2,512,3,64]{1,0,3,2:T(2,128)(2,1)}, bf16[2,512,3,64]{1,0,3,2:T(2,128)(2,1)S(1)}, u32[]{:S(2)}) copy-start(bf16[2,512,3,64]{1,0,3,2:T(2,128)(2,1)S(1)} %get-tuple-element.165) | copy-start | bytes 1179652
  99.2 4.5 copy-start
  99.2 4.7 copy-start.39
  104.0 3.3 copy-start.40
  104.0 3.3 copy-start.22
  104.0 3.3 copy-start.26
  108.7 2.9 copy-start.1
  108.7 2.9 copy-start.41
  117.4 109.6 %copy-start.2 = (bf16[512,768]{1,0:T(8,128)(2,1)S(1)}, bf16[512,768]{1,0:T(8,128)(2,1)}, u32[]{:S(2)}) copy-start(bf16[512,768]{1,0:T(8,128)(2,1)} %param.30) | copy-start | bytes 2359300
  117.4 226.5 %all-gather.10.cloned.1.call-start = ((), (), s32[]{:S(2)}) async-start(), calls=%async_computation.13 | async-start | bytes 1327104 | tf_op jit(solution)/shard_map/all_gather | solution.py:172
  118.0 225.9 %all-gather.8.cloned.1.call-start = ((), (), s32[]{:S(2)}) async-start(), calls=%async_computation.12 | async-start | bytes 3932160 | tf_op jit(solution)/shard_map/all_gather | solution.py:206
  118.7 111.6 %copy-start.5 = (bf16[512,768]{1,0:T(8,128)(2,1)S(1)}, bf16[512,768]{1,0:T(8,128)(2,1)}, u32[]{:S(2)}) copy-start(bf16[512,768]{1,0:T(8,128)(2,1)} %param.32) | copy-start | bytes 2359300
  230.3 133.1 %all-gather.12.cloned.1.call-start = ((), (), s32[]{:S(2)}) async-start(), calls=%async_computation.14 | async-start | bytes 1327104 | tf_op jit(solution)/shard_map/all_gather | solution.py:173
  230.3 37.7 %collective-permute-start = (bf16[512,768]{1,0:T(8,128)(2,1)S(1)}, bf16[512,768]{1,0:T(8,128)(2,1)S(1)}, u32[]{:S(2)}, u32[]{:S(2)}) collective-permute-start(bf16[512,768]{1,0:T(8,128)(2,1)S(1)} %copy-done.5), channel_id=1, source_target_pairs={{0,3},{1,0},{2,1},{3,2},{4,7},{5,4},{6,5},{7,6},{8,11},{9,8},{10,9... | collective-permute-start | bytes 2359304 | tf_op jit(solution)/shard_map/ppermute | solution.py:221
  268.9 48.2 %collective-permute-start.1 = (bf16[512,768]{1,0:T(8,128)(2,1)S(1)}, bf16[512,768]{1,0:T(8,128)(2,1)}, u32[]{:S(2)}, u32[]{:S(2)}) collective-permute-start(bf16[512,768]{1,0:T(8,128)(2,1)S(1)} %collective-permute-done), channel_id=1, source_target_pairs={{0,3},{1,0},{2,1},{3,2},{4,7},{5,4},{6,5},{7,6},{8,11},{9,8},{10,9... | collective-permute-start | bytes 2359304 | tf_op jit(solution)/shard_map/ppermute | solution.py:221
  317.1 18.7 %collective-permute-start.2 = (bf16[512,768]{1,0:T(8,128)(2,1)}, bf16[512,768]{1,0:T(8,128)(2,1)}, u32[]{:S(2)}, u32[]{:S(2)}) collective-permute-start(bf16[512,768]{1,0:T(8,128)(2,1)} %collective-permute-done.1), channel_id=1, source_target_pairs={{0,3},{1,0},{2,1},{3,2},{4,7},{5,4},{6,5},{7,6},{8,11},{9,8},{10,9... | collective-permute-start | bytes 2359304 | tf_op jit(solution)/shard_map/ppermute | solution.py:221
  317.1 174.9 %reduce-scatter.23.cloned.1.call-start = ((), (), s32[]{:S(2)}) async-start(), calls=%async_computation.16 | async-start | bytes 7864320 | tf_op jit(solution)/shard_map/reduce_scatter | solution.py:236
  317.2 21.6 %copy-start.15 = (bf16[512,768]{1,0:T(8,128)(2,1)S(1)}, bf16[512,768]{1,0:T(8,128)(2,1)}, u32[]{:S(2)}) copy-start(bf16[512,768]{1,0:T(8,128)(2,1)} %copy-done.14) | copy-start | bytes 2359300
  363.3 12.7 %copy-start.60 = (bf16[768,768]{1,0:T(8,128)(2,1)S(1)}, bf16[768,768]{1,0:T(8,128)(2,1)}, u32[]{:S(2)}) copy-start(bf16[768,768]{1,0:T(8,128)(2,1)} %all-gather.10.cloned.1.call-done) | copy-start | bytes 3538948
  380.6 174.7 %reduce-scatter.21.cloned.1.call-start = ((), (), s32[]{:S(2)}) async-start(), calls=%async_computation.15 | async-start | bytes 3932160 | tf_op jit(solution)/shard_map/reduce_scatter | solution.py:209
  387.3 237.0 %all-gather.14.cloned.1.call-start = ((), (), s32[]{:S(2)}) async-start(), calls=%async_computation.17 | async-start | bytes 3932160 | tf_op jit(solution)/shard_map/all_gather | solution.py:241
  560.8 148.1 %reduce-scatter.37.cloned.1.call-start = ((), (), s32[]{:S(2)}) async-start(), calls=%async_computation.24 | async-start | bytes 884736
  627.9 4.6 copy-start.21
  627.9 4.6 copy-start.33
  628.5 8.5 slice-start.3
  632.5 4.4 slice-start.4
  632.5 4.4 copy-start.34
  638.8 4.4 copy-start.11
  638.9 4.4 copy-start.16
  645.5 96.3 %reduce-scatter.25.cloned.1.call-start = ((), (), s32[]{:S(2)}) async-start(), calls=%async_computation.18 | async-start | bytes 3932160 | tf_op jit(solution)/shard_map/reduce_scatter | solution.py:257
  645.8 17.7 %slice-start = ((s8[12582912]{0:T(1024)(128)(4,1)}), s8[4194304]{0:T(1024)(128)(4,1)S(1)}, s32[]{:S(2)}) async-start(s8[12582912]{0:T(1024)(128)(4,1)} %bitcast.78), calls=%async_computation.25 | async-start | bytes 8388608
  645.8 17.7 %slice-start.1 = ((s8[12582912]{0:T(1024)(128)(4,1)}), s8[4194304]{0:T(1024)(128)(4,1)S(1)}, s32[]{:S(2)}) async-start(s8[12582912]{0:T(1024)(128)(4,1)} %bitcast.78), calls=%async_computation.26 | async-start | bytes 8388608
  656.4 7.1 slice-start.2
  663.5 6.4 copy-start.9
  674.4 2.7 copy-start.28
  681.6 108.5 %reduce-scatter.27.cloned.1.call-start = ((), (), s32[]{:S(2)}) async-start(), calls=%async_computation.19 | async-start | bytes 2654208 | tf_op jit(solution)/shard_map/reduce_scatter | solution.py:273
  688.9 145.3 %reduce-scatter.29.cloned.1.call-start = ((), (), s32[]{:S(2)}) async-start(), calls=%async_computation.20 | async-start | bytes 2654208 | tf_op jit(solution)/shard_map/reduce_scatter | solution.py:274
  695.9 177.0 %reduce-scatter.35.cloned.1.call-start = ((), (), s32[]{:S(2)}) async-start(), calls=%async_computation.23 | async-start | bytes 884736
  700.6 3.4 copy-start.55
  702.6 39.2 %copy-start.36 = (f32[768]{0:T(1024)S(1)}, f32[768]{0:T(1024)}, u32[]{:S(2)}) copy-start(f32[768]{0:T(1024)} %copy-done.35) | copy-start | bytes 9220
  702.6 39.2 %copy-start.38 = (f32[512]{0:T(512)S(1)}, f32[512]{0:T(512)}, u32[]{:S(2)}) copy-start(f32[512]{0:T(512)} %copy-done.37) | copy-start | bytes 6148
  702.7 208.7 %reduce-scatter.33.cloned.1.call-start = ((), (), s32[]{:S(2)}) async-start(), calls=%async_computation.22 | async-start | bytes 884736
  702.7 40.8 %copy-start.49 = (f32[512]{0:T(512)S(1)}, f32[512]{0:T(512)}, u32[]{:S(2)}) copy-start(f32[512]{0:T(512)} %copy-done.48) | copy-start | bytes 6148
  702.7 40.8 %copy-start.47 = (f32[512]{0:T(512)S(1)}, f32[512]{0:T(512)}, u32[]{:S(2)}) copy-start(f32[512]{0:T(512)} %copy-done.46) | copy-start | bytes 6148
  703.9 41.7 %copy-start.4 = (f32[512,768]{1,0:T(8,128)S(1)}, f32[512,768]{1,0:T(8,128)}, u32[]{:S(2)}) copy-start(f32[512,768]{1,0:T(8,128)} %copy-done.3) | copy-start | bytes 4718596
  703.9 41.7 %copy-start.51 = (f32[512]{0:T(512)S(1)}, f32[512]{0:T(512)}, u32[]{:S(2)}) copy-start(f32[512]{0:T(512)} %copy-done.50) | copy-start | bytes 6148
  703.9 246.2 %reduce-scatter.31.cloned.1.call-start = ((), (), s32[]{:S(2)}) async-start(), calls=%async_computation.21 | async-start | bytes 884736
  710.6 38.2 %copy-start.53 = (f32[768]{0:T(1024)S(1)}, f32[768]{0:T(1024)}, u32[]{:S(2)}) copy-start(f32[768]{0:T(1024)} %get-tuple-element.132) | copy-start | bytes 9220
  710.6 38.2 %copy-start.54 = (f32[768]{0:T(1024)S(1)}, f32[768]{0:T(1024)}, u32[]{:S(2)}) copy-start(f32[768]{0:T(1024)} %get-tuple-element.136) | copy-start | bytes 9220
  (21 other events, 32.0 us)
Sparse Core Ops, SparseCore 0:
  15.4 66.1 all-gather.5
  117.5 109.4 reduce-scatter.18
  560.9 63.2 all-gather.13
Sparse Core Ops, SparseCore 1:
  119.8 22.4 all-gather.9
  230.3 87.6 all-gather.7
  319.8 25.8 all-gather.11
  380.7 111.3 reduce-scatter.22
  494.3 60.9 reduce-scatter.20
  645.6 33.5 reduce-scatter.36
  681.7 60.0 reduce-scatter.24
  745.6 42.3 reduce-scatter.26
  791.7 42.4 reduce-scatter.28
  837.9 34.9 reduce-scatter.34
  876.5 34.9 reduce-scatter.32
  915.2 34.9 reduce-scatter.30
